TPU v7x, 512 devices: a whole 4x4x16 slice. The times are simulated.
512 devices in a mesh: ctx: 32 (over x, y, core), head: 16 (over z).
Axes of the slice: x: 4, y: 4, z: 16, core: 2. Of those that a mesh axis runs over, the one named last changes fastest.
Arguments:
- q_linear: bfloat16 [8192, 8192], P('ctx', 'head'), may hold values from -4 to 4
- k_linear: bfloat16 [8192, 8192], P('ctx', 'head'), may hold values from -4 to 4
- v_linear: bfloat16 [8192, 8192], P('ctx', 'head'), may hold values from -40 to 40
- log_decay: float32 [8192, 64], P('ctx', 'head'), may hold values from -1 to 0
- norm_gain: float32 [8192], P('head'), may hold values from 0.5 to 1.5
- q_soft: bfloat16 [8192, 8192], P('ctx', 'head'), may hold values from -6 to 6
- k_soft: bfloat16 [8192, 1024], P('ctx'), may hold values from -4 to 4
- v_soft: bfloat16 [8192, 1024], P('ctx'), may hold values from -4 to 4
Outputs:
- linear_out: bfloat16 [8192, 8192], P('ctx', 'head')
- soft_out: bfloat16 [8192, 8192], P('ctx', 'head')
All inputs are finite; a program needn't handle non-finite values.
Results may differ from a plain program's by a relative error of at most 0.0075.
Values may be sent and summed in bfloat16 or wider, within the bound.
No kernel may reach another device: no remote copies, remote signals or barrier semaphores. Data moves between devices by JAX's collectives and lax.ppermute only.
A program may use at most 64 MiB of HBM per device.

v0:
```python
import jax
import jax.numpy as jnp
from jax import lax
from jax.experimental import pallas as pl
from jax.experimental.pallas import tpu as pltpu
from jax.sharding import PartitionSpec as P

import numpy as np

QUERY_HEADS = 64
DH = 128
KV_HEADS = 8
BLOCK = 256
KEY_BLOCK = 512
HEAD_AXES = ("head_hi", "head_lo")


EPSILON = 1e-06
NEGATIVE = -1e30


def shifted(value, axis, steps):
    count = lax.axis_size(axis)
    first, last = (max(0, -steps), min(count, count - steps))
    return lax.ppermute(value, axis, [(source, source + steps) for source in range(first, last)])


def lightning_step(carry, inputs):
    running, log_before = carry
    queries, key_rows, value_rows, log_gates = inputs
    row_count = queries.shape[0]
    cumulative = jnp.cumsum(log_gates, axis=0)
    final_log = cumulative[-1]
    positions = jnp.arange(row_count, dtype=jnp.int32)
    causal = positions[None, :] <= positions[:, None]
    cum_heads = cumulative.T
    log_gap = jnp.where(causal[None], cum_heads[:, :, None] - cum_heads[:, None, :], NEGATIVE)
    scores = jnp.einsum("thd,shd->hts", queries, key_rows, preferred_element_type=jnp.float32)
    weights = (scores * jnp.exp(log_gap)).astype(jnp.bfloat16)
    intra_part = jnp.einsum("hts,she->the", weights, value_rows, preferred_element_type=jnp.float32)
    query_wide = queries.astype(jnp.float32)
    lifted_here = query_wide * jnp.exp(cumulative)[:, :, None]
    carried_here = jnp.einsum("thd,hde->the", lifted_here, running, precision=lax.Precision.HIGHEST)
    lifted_device = query_wide * jnp.exp(cumulative + log_before[None, :])[:, :, None]
    scaled = (key_rows * jnp.exp(final_log[None, :] - cumulative)[:, :, None]).astype(jnp.bfloat16)
    block_state = jnp.einsum("shd,she->hde", scaled, value_rows, preferred_element_type=jnp.float32)
    running = jnp.exp(final_log)[:, None, None] * running + block_state
    return ((running, log_before + final_log), (intra_part + carried_here, lifted_device))


def exclusive_scan(log_total, block_state, axis):
    head_count, rows, cols = block_state.shape

    def pack(log, state):
        return jnp.concatenate(
            [state, jnp.broadcast_to(log[:, None, None], (head_count, 8, cols))], axis=1
        )

    count = lax.axis_size(axis)
    window_log, window_state = None, None
    step = 1
    while step < count:
        if window_log is None:
            sent_log, sent_state = log_total, block_state
        else:
            sent_state = jnp.exp(log_total)[:, None, None] * window_state + block_state
            sent_log = window_log + log_total
        incoming = shifted(pack(sent_log, sent_state), axis, step)
        incoming_log, incoming_state = incoming[:, rows, 0], incoming[:, :rows]
        if window_log is None:
            window_log, window_state = incoming_log, incoming_state
        else:
            window_state = jnp.exp(window_log)[:, None, None] * incoming_state + window_state
            window_log = window_log + incoming_log
        step *= 2
    return window_state


def split_sum(value):
    partial = lax.optimization_barrier(lax.psum(value, "head_lo"))
    return lax.psum(partial, "head_hi")


def soft_kernel(index_ref, q_ref, kvt_ref, o_ref, max_ref, total_ref, acc_ref):
    my_index = index_ref[0]
    row_count = o_ref.shape[0]
    head_count = o_ref.shape[1] // DH
    wide = q_ref.shape[0]
    max_ref[...] = jnp.full(max_ref.shape, NEGATIVE, jnp.float32)
    total_ref[...] = jnp.zeros(total_ref.shape, jnp.float32)
    acc_ref[...] = jnp.zeros(acc_ref.shape, jnp.float32)
    full_blocks = (my_index * row_count) // KEY_BLOCK
    block_count = (my_index * row_count + row_count - 1) // KEY_BLOCK + 1

    def update(block, masked):
        start = pl.multiple_of(block * KEY_BLOCK, KEY_BLOCK)
        keys_t = kvt_ref[0:DH, pl.ds(start, KEY_BLOCK)]
        values_t = kvt_ref[DH : 2 * DH, pl.ds(start, KEY_BLOCK)]
        scores = lax.dot_general(
            keys_t, q_ref[...], (((0,), (1,)), ((), ())), preferred_element_type=jnp.float32
        ) * DH ** (-0.5)
        if masked:
            key_pos = start + lax.broadcasted_iota(jnp.int32, (KEY_BLOCK, wide), 0)
            query_pos = my_index * row_count + lax.rem(
                lax.broadcasted_iota(jnp.int32, (KEY_BLOCK, wide), 1), row_count
            )
            allowed = key_pos <= query_pos
            scores = jnp.where(allowed, scores, NEGATIVE)
        row_max = max_ref[...]
        new_max = jnp.maximum(row_max, jnp.max(scores, axis=0, keepdims=True))
        probabilities = jnp.exp(scores - new_max)
        if masked:
            probabilities = jnp.where(allowed, probabilities, 0.0)
        rescale = jnp.exp(row_max - new_max)
        total_ref[...] = total_ref[...] * rescale + jnp.sum(probabilities, axis=0, keepdims=True)
        product = jnp.dot(
            values_t, probabilities.astype(jnp.bfloat16), preferred_element_type=jnp.float32
        )
        acc_ref[...] = acc_ref[...] * rescale + product
        max_ref[...] = new_max

    def plain(block, carry):
        update(block, False)
        return carry

    def diagonal(block, carry):
        update(block, True)
        return carry

    lax.fori_loop(0, full_blocks, plain, 0)
    lax.fori_loop(full_blocks, block_count, diagonal, 0)
    for head in range(head_count):
        cols = slice(head * row_count, (head + 1) * row_count)
        ratio = acc_ref[:, cols] / total_ref[:, cols]
        o_ref[:, head * DH : (head + 1) * DH] = ratio.T.astype(o_ref.dtype)


def soft_attention(my_index, queries, keys_values):
    row_count, width = queries.shape
    head_count = width // DH
    wide = head_count * row_count
    stacked = queries.reshape(row_count, head_count, DH).transpose(1, 0, 2).reshape(wide, DH)
    keys_values_t = keys_values.T
    return pl.pallas_call(
        soft_kernel,
        out_shape=jax.ShapeDtypeStruct((row_count, width), jnp.bfloat16),
        in_specs=[
            pl.BlockSpec(memory_space=pltpu.SMEM),
            pl.BlockSpec(memory_space=pltpu.VMEM),
            pl.BlockSpec(memory_space=pltpu.VMEM),
        ],
        out_specs=pl.BlockSpec(memory_space=pltpu.VMEM),
        scratch_shapes=[
            pltpu.VMEM((1, wide), jnp.float32),
            pltpu.VMEM((1, wide), jnp.float32),
            pltpu.VMEM((DH, wide), jnp.float32),
        ],
    )(my_index.reshape(1), stacked, keys_values_t)


def layer(q_linear, k_linear, v_linear, log_decay, norm_gain, q_soft, k_soft, v_soft):
    row_count = q_linear.shape[0]
    head_count = log_decay.shape[1]
    width = head_count * DH
    group_size = QUERY_HEADS // KV_HEADS
    kv_count = max(1, head_count // group_size)
    kv_start = lax.axis_index(HEAD_AXES) * head_count // group_size
    k_local = lax.dynamic_slice_in_dim(k_soft, kv_start * DH, kv_count * DH, 1)
    v_local = lax.dynamic_slice_in_dim(v_soft, kv_start * DH, kv_count * DH, 1)
    keys_values = lax.all_gather(
        jnp.concatenate([k_local, v_local], axis=1), "ctx", axis=0, tiled=True
    )

    local_blocks = row_count // BLOCK
    lin_shape = (local_blocks, BLOCK, head_count, DH)
    sequences = (
        q_linear.reshape(lin_shape),
        k_linear.reshape(lin_shape),
        v_linear.reshape(lin_shape),
        log_decay.reshape(local_blocks, BLOCK, head_count),
    )
    start_carry = (
        jnp.zeros((head_count, DH, DH), jnp.float32),
        jnp.zeros((head_count,), jnp.float32),
    )
    (block_state, log_total), (local_part, lifted) = lax.scan(
        lightning_step, start_carry, sequences
    )
    local_part = local_part.reshape(row_count, head_count, DH)
    lifted = lifted.reshape(row_count, head_count, DH)
    entering = exclusive_scan(log_total, block_state, "ctx")
    carried = jnp.einsum("thd,hde->the", lifted, entering, precision=lax.Precision.HIGHEST)
    mixed = (local_part + carried).reshape(row_count, width)
    power = split_sum(jnp.sum(mixed * mixed, axis=1)) / (QUERY_HEADS * DH)
    linear_out = (mixed * lax.rsqrt(power + EPSILON)[:, None] * norm_gain[None, :]).astype(
        jnp.bfloat16
    )

    my_index = lax.axis_index("ctx").astype(jnp.int32)
    if kv_count == 1:
        soft_out = soft_attention(my_index, q_soft, keys_values)
    else:
        raise NotImplementedError("kv_count > 1")
    return (linear_out, soft_out)


def solution(mesh):
    ctx_count, head_count = mesh.devices.shape
    low = 4 if head_count % 4 == 0 else 1
    split = jax.sharding.Mesh(
        np.asarray(mesh.devices).reshape(ctx_count, head_count // low, low), ("ctx",) + HEAD_AXES
    )
    return jax.shard_map(
        layer,
        mesh=split,
        in_specs=(
            P("ctx", HEAD_AXES),
            P("ctx", HEAD_AXES),
            P("ctx", HEAD_AXES),
            P("ctx", HEAD_AXES),
            P(HEAD_AXES),
            P("ctx", HEAD_AXES),
            P("ctx", None),
            P("ctx", None),
        ),
        out_specs=(P("ctx", HEAD_AXES), P("ctx", HEAD_AXES)),
        check_vma=False,
    )
```

profile of v0, /device:TPU:6, one launch (start us, length us, event | category | flops | bytes accessed | tf_op | source)
XLA Modules:
  0.0 127.2 jit_solution(7962073977891268542)
XLA Ops:
  7.2 0.0 all-gather.2.cloned.1.call-start
  7.3 0.9 constant_dynamic-slice_fusion
  8.2 0.1 copy.81
  8.3 0.1 copy.82
  8.4 0.7 pad_maximum_fusion.5
  9.1 0.0 all-gather.2.cloned.1.call-update
  9.1 0.7 reshape.90
  9.8 1.2 reduce-window.6
  11.0 0.1 slice.49
  11.1 0.1 copy.65
  11.2 0.1 copy.66
  11.3 0.1 add_bitcast_fusion
  11.4 1.1 copy.83
  12.5 0.2 fusion.37
  12.7 0.1 subtract_exponential_fusion
  12.8 1.2 convolution_add_fusion
  14.0 0.1 broadcast_in_dim.98
  14.1 1.9 %collective-permute-start = (f32[4,136,128]{2,1,0:T(8,128)S(1)}, f32[4,136,128]{2,1,0:T(8,128)S(1)}, u32[]{:S(2)}, u32[]{:S(2)}) collective-permute-start(f32[4,136,128]{2,1,0:T(8,128)S(1)} %pad_maximum_fusion), channel_id=1, source_target_pairs={{0,16},{16,32},{32,48},{48,64},{64,80},{80,96},{96,112},{112,128},... | collective-permute-start | bytes 835592 | tf_op jit(solution)/shard_map/ppermute | solution.py:25
  16.0 8.0 %collective-permute-done = f32[4,136,128]{2,1,0:T(8,128)S(1)} collective-permute-done((f32[4,136,128]{2,1,0:T(8,128)S(1)}, f32[4,136,128]{2,1,0:T(8,128)S(1)}, u32[]{:S(2)}, u32[]{:S(2)}) %collective-permute-start) | collective-permute-done | bytes 278560 | tf_op jit(solution)/shard_map/ppermute | solution.py:25
  24.0 0.1 exponential_reduce_fusion.3
  24.2 0.1 multiply_add_fusion.3
  24.3 0.1 broadcast_in_dim.100
  24.4 1.9 %collective-permute-start.1 = (f32[4,136,128]{2,1,0:T(8,128)S(1)}, f32[4,136,128]{2,1,0:T(8,128)S(1)}, u32[]{:S(2)}, u32[]{:S(2)}) collective-permute-start(f32[4,136,128]{2,1,0:T(8,128)S(1)} %pad_maximum_fusion.1), channel_id=1, source_target_pairs={{0,32},{16,48},{32,64},{48,80},{64,96},{80,112},{96,128},{112,144}... | collective-permute-start | bytes 835592 | tf_op jit(solution)/shard_map/ppermute | solution.py:25
  26.3 8.6 %collective-permute-done.1 = f32[4,136,128]{2,1,0:T(8,128)S(1)} collective-permute-done((f32[4,136,128]{2,1,0:T(8,128)S(1)}, f32[4,136,128]{2,1,0:T(8,128)S(1)}, u32[]{:S(2)}, u32[]{:S(2)}) %collective-permute-start.1) | collective-permute-done | bytes 278560 | tf_op jit(solution)/shard_map/ppermute | solution.py:25
  34.9 0.1 exponential_reduce_fusion.2
  35.0 0.1 multiply_add_fusion.2
  35.2 0.1 broadcast_in_dim.102
  35.3 1.9 %collective-permute-start.2 = (f32[4,136,128]{2,1,0:T(8,128)S(1)}, f32[4,136,128]{2,1,0:T(8,128)S(1)}, u32[]{:S(2)}, u32[]{:S(2)}) collective-permute-start(f32[4,136,128]{2,1,0:T(8,128)S(1)} %pad_maximum_fusion.2), channel_id=1, source_target_pairs={{0,64},{16,80},{32,96},{48,112},{64,128},{80,144},{96,160},{112,17... | collective-permute-start | bytes 835592 | tf_op jit(solution)/shard_map/ppermute | solution.py:25
  37.2 10.1 %collective-permute-done.2 = f32[4,136,128]{2,1,0:T(8,128)S(1)} collective-permute-done((f32[4,136,128]{2,1,0:T(8,128)S(1)}, f32[4,136,128]{2,1,0:T(8,128)S(1)}, u32[]{:S(2)}, u32[]{:S(2)}) %collective-permute-start.2) | collective-permute-done | bytes 278560 | tf_op jit(solution)/shard_map/ppermute | solution.py:25
  47.2 0.1 add_reduce_fusion.1
  47.4 0.1 multiply_add_fusion.1
  47.5 0.1 broadcast_in_dim.104
  47.6 1.3 %collective-permute-start.3 = (f32[4,136,128]{2,1,0:T(8,128)S(1)}, f32[4,136,128]{2,1,0:T(8,128)S(1)}, u32[]{:S(2)}, u32[]{:S(2)}) collective-permute-start(f32[4,136,128]{2,1,0:T(8,128)S(1)} %pad_maximum_fusion.3), channel_id=1, source_target_pairs={{0,128},{16,144},{32,160},{48,176},{64,192},{80,208},{96,224},{112... | collective-permute-start | bytes 835592 | tf_op jit(solution)/shard_map/ppermute | solution.py:25
  48.9 0.7 copy_bitcast_fusion
  49.6 0.7 convolution_bitcast_fusion.1
  50.4 5.7 %collective-permute-done.3 = f32[4,136,128]{2,1,0:T(8,128)S(1)} collective-permute-done((f32[4,136,128]{2,1,0:T(8,128)S(1)}, f32[4,136,128]{2,1,0:T(8,128)S(1)}, u32[]{:S(2)}, u32[]{:S(2)}) %collective-permute-start.3) | collective-permute-done | bytes 278560 | tf_op jit(solution)/shard_map/ppermute | solution.py:25
  56.0 0.1 exponential_reduce_fusion.1
  56.1 0.1 multiply_add_fusion
  56.3 0.1 broadcast_in_dim.106
  56.4 1.3 %collective-permute-start.4 = (f32[4,136,128]{2,1,0:T(8,128)S(1)}, f32[4,136,128]{2,1,0:T(8,128)S(1)}, u32[]{:S(2)}, u32[]{:S(2)}) collective-permute-start(f32[4,136,128]{2,1,0:T(8,128)S(1)} %pad_maximum_fusion.4), channel_id=1, source_target_pairs={{0,256},{16,272},{32,288},{48,304},{64,320},{80,336},{96,352},{112... | collective-permute-start | bytes 835592 | tf_op jit(solution)/shard_map/ppermute | solution.py:25
  57.7 0.6 fusion.1
  58.3 8.0 %collective-permute-done.4 = f32[4,136,128]{2,1,0:T(8,128)S(1)} collective-permute-done((f32[4,136,128]{2,1,0:T(8,128)S(1)}, f32[4,136,128]{2,1,0:T(8,128)S(1)}, u32[]{:S(2)}, u32[]{:S(2)}) %collective-permute-start.4) | collective-permute-done | bytes 278560 | tf_op jit(solution)/shard_map/ppermute | solution.py:25
  66.3 0.8 multiply_reduce_fusion
  67.1 0.2 copy.76
  67.3 12.3 %psum.14 = f32[256]{0:T(256)S(1)} all-reduce(f32[256]{0:T(256)S(1)} %get-tuple-element.51), channel_id=1, replica_groups=mesh['ctx'=32,'head_hi'=4,'head_lo'=4] {'head_lo'}, use_global_device_ids=true, to_apply=%region_3.4 | all-reduce | flops 256 | bytes 2048 | tf_op jit(solution)/shard_map/psum | solution.py:80
  79.6 21.3 %psum.15 = f32[256]{0:T(256)S(1)} all-reduce(f32[256]{0:T(256)S(1)} %psum.14), channel_id=1, replica_groups=mesh['ctx'=32,'head_hi'=4,'head_lo'=4] {'head_hi'}, use_global_device_ids=true, to_apply=%region_4.5 | all-reduce | flops 256 | bytes 2048 | tf_op jit(solution)/shard_map/psum | solution.py:81
  100.9 0.8 multiply_convert_fusion
  101.7 18.6 %shard_map.95 = bf16[256,512]{1,0:T(8,128)(2,1)} custom-call(s32[1]{0:T(128)} %bitcast.11.index_ref, bf16[1024,128]{1,0:T(8,128)(2,1)} %bitcast.84, bf16[256,8192]{1,0:T(8,128)(2,1)} %bitcast.82), custom_call_target="tpu_custom_call" | custom-call | tf_op jit(solution)/shard_map/pallas_call | solution.py:144
  (20 shorter events, 0.2 us)
Async XLA Ops:
  7.2 42.4 %copy-start = (bf16[256,512]{1,0:T(8,128)(2,1)S(1)}, bf16[256,512]{1,0:T(8,128)(2,1)}, u32[]{:S(2)}) copy-start(bf16[256,512]{1,0:T(8,128)(2,1)} %param.8) | copy-start | bytes 786436
  7.2 41.7 %copy-start.1 = (bf16[256,512]{1,0:T(8,128)(2,1)S(1)}, bf16[256,512]{1,0:T(8,128)(2,1)}, u32[]{:S(2)}) copy-start(bf16[256,512]{1,0:T(8,128)(2,1)} %param.13) | copy-start | bytes 786436
  7.2 94.5 %all-gather.2.cloned.1.call-start = ((), (), s32[]{:S(2)}) async-start(), calls=%async_computation | async-start | bytes 4325376 | tf_op jit(solution)/shard_map/all_gather | solution.py:170
  14.1 10.0 %collective-permute-start = (f32[4,136,128]{2,1,0:T(8,128)S(1)}, f32[4,136,128]{2,1,0:T(8,128)S(1)}, u32[]{:S(2)}, u32[]{:S(2)}) collective-permute-start(f32[4,136,128]{2,1,0:T(8,128)S(1)} %pad_maximum_fusion), channel_id=1, source_target_pairs={{0,16},{16,32},{32,48},{48,64},{64,80},{80,96},{96,112},{112,128},... | collective-permute-start | bytes 835592 | tf_op jit(solution)/shard_map/ppermute | solution.py:25
  24.2 33.6 %copy-start.2 = (bf16[256,512]{1,0:T(8,128)(2,1)S(1)}, bf16[256,512]{1,0:T(8,128)(2,1)}, u32[]{:S(2)}) copy-start(bf16[256,512]{1,0:T(8,128)(2,1)} %param.10) | copy-start | bytes 786436
  24.4 10.6 %collective-permute-start.1 = (f32[4,136,128]{2,1,0:T(8,128)S(1)}, f32[4,136,128]{2,1,0:T(8,128)S(1)}, u32[]{:S(2)}, u32[]{:S(2)}) collective-permute-start(f32[4,136,128]{2,1,0:T(8,128)S(1)} %pad_maximum_fusion.1), channel_id=1, source_target_pairs={{0,32},{16,48},{32,64},{48,80},{64,96},{80,112},{96,128},{112,144}... | collective-permute-start | bytes 835592 | tf_op jit(solution)/shard_map/ppermute | solution.py:25
  35.3 12.0 %collective-permute-start.2 = (f32[4,136,128]{2,1,0:T(8,128)S(1)}, f32[4,136,128]{2,1,0:T(8,128)S(1)}, u32[]{:S(2)}, u32[]{:S(2)}) collective-permute-start(f32[4,136,128]{2,1,0:T(8,128)S(1)} %pad_maximum_fusion.2), channel_id=1, source_target_pairs={{0,64},{16,80},{32,96},{48,112},{64,128},{80,144},{96,160},{112,17... | collective-permute-start | bytes 835592 | tf_op jit(solution)/shard_map/ppermute | solution.py:25
  47.6 8.4 %collective-permute-start.3 = (f32[4,136,128]{2,1,0:T(8,128)S(1)}, f32[4,136,128]{2,1,0:T(8,128)S(1)}, u32[]{:S(2)}, u32[]{:S(2)}) collective-permute-start(f32[4,136,128]{2,1,0:T(8,128)S(1)} %pad_maximum_fusion.3), channel_id=1, source_target_pairs={{0,128},{16,144},{32,160},{48,176},{64,192},{80,208},{96,224},{112... | collective-permute-start | bytes 835592 | tf_op jit(solution)/shard_map/ppermute | solution.py:25
  49.6 51.3 %copy-start.3 = (f32[512]{0:T(512)S(1)}, f32[512]{0:T(512)}, u32[]{:S(2)}) copy-start(f32[512]{0:T(512)} %param.12) | copy-start | bytes 6148
  56.4 9.9 %collective-permute-start.4 = (f32[4,136,128]{2,1,0:T(8,128)S(1)}, f32[4,136,128]{2,1,0:T(8,128)S(1)}, u32[]{:S(2)}, u32[]{:S(2)}) collective-permute-start(f32[4,136,128]{2,1,0:T(8,128)S(1)} %pad_maximum_fusion.4), channel_id=1, source_target_pairs={{0,256},{16,272},{32,288},{48,304},{64,320},{80,336},{96,352},{112... | collective-permute-start | bytes 835592 | tf_op jit(solution)/shard_map/ppermute | solution.py:25
Sparse Core Ops, SparseCore 0:
  11.6 72.3 all-gather.1
where the time goes:
time: 128 us; the launch traced here: 127 us
  waiting for transfers between devices  40.4 us (32%)
  blocking collectives  33.6 us (26%)
  Pallas kernels  18.6 us (15%)
  between operations  14.3 us (11%)
  starting transfers between devices  8.38 us (7%)
  local copies, waits for them, and re-layouts  4.7 us (4%)
  other arithmetic  3.97 us (3%)
  matrix products  3.28 us (3%)
    ppermute x5, waiting for transfers between devices, shifted(): lax.ppermute(value, axis, [(source, source + steps) for source in range(f...  40.4 us
    psum x1, blocking collectives, split_sum(): return lax.psum(partial, 'head_hi')  21.3 us
    pallas_call x1, Pallas kernels, soft_attention(): pl.pallas_call(soft_kernel, out_shape=jax.ShapeDtypeStruct((row_count, wi...  18.6 us
    psum x1, blocking collectives, split_sum(): partial = lax.optimization_barrier(lax.psum(value, 'head_lo'))  12.3 us
    ppermute x5, starting transfers between devices, shifted(): lax.ppermute(value, axis, [(source, source + steps) for source in range(f...  8.35 us
  transfers between devices with their start and end apart: 6, of which 5 were waited for; matrix products, arithmetic and copies ran while one was open for 8% of the time, Pallas kernels for 0%

commit v1 on v0

--- a/solution.py
+++ b/solution.py
@@ -12,7 +12,7 @@
 KV_HEADS = 8
 BLOCK = 256
 KEY_BLOCK = 512
-HEAD_AXES = ("head_hi", "head_lo")
+HEAD_AXES = ("head_8", "head_4", "head_2", "head_1")
 
 
 EPSILON = 1e-06
@@ -77,8 +77,9 @@
 
 
 def split_sum(value):
-    partial = lax.optimization_barrier(lax.psum(value, "head_lo"))
-    return lax.psum(partial, "head_hi")
+    for axis in reversed(HEAD_AXES):
+        value = lax.psum(value, axis)
+    return value
 
 
 def soft_kernel(index_ref, q_ref, kvt_ref, o_ref, max_ref, total_ref, acc_ref):
@@ -206,9 +207,9 @@
 
 def solution(mesh):
     ctx_count, head_count = mesh.devices.shape
-    low = 4 if head_count % 4 == 0 else 1
+    assert head_count == 2 ** len(HEAD_AXES)
     split = jax.sharding.Mesh(
-        np.asarray(mesh.devices).reshape(ctx_count, head_count // low, low), ("ctx",) + HEAD_AXES
+        np.asarray(mesh.devices).reshape((ctx_count,) + (2,) * len(HEAD_AXES)), ("ctx",) + HEAD_AXES
     )
     return jax.shard_map(
         layer,

time: 128 us -> 131 us (1.023)
  blocking collectives: 33.6 us -> 37.4 us
    psum x2 -> x4, blocking collectives: 33.6 us -> 37.4 us  [split_sum(): value = lax.psum(value, axis)]
where the time goes in v1:
time: 131 us
  waiting for transfers between devices  40.2 us (31%)
  blocking collectives  37.4 us (29%)
  Pallas kernels  18.6 us (14%)
  between operations  14.3 us (11%)
  starting transfers between devices  8.38 us (6%)
  local copies, waits for them, and re-layouts  4.7 us (4%)
  other arithmetic  3.97 us (3%)
  matrix products  3.28 us (3%)
    ppermute x5, waiting for transfers between devices, shifted(): lax.ppermute(value, axis, [(source, source + steps) for source in range(f...  40.2 us
    psum x4, blocking collectives, split_sum(): value = lax.psum(value, axis)  37.4 us
    pallas_call x1, Pallas kernels, soft_attention(): pl.pallas_call(soft_kernel, out_shape=jax.ShapeDtypeStruct((row_count, wi...  18.6 us
    ppermute x5, starting transfers between devices, shifted(): lax.ppermute(value, axis, [(source, source + steps) for source in range(f...  8.35 us
  transfers between devices with their start and end apart: 6, of which 5 were waited for; matrix products, arithmetic and copies ran while one was open for 8% of the time, Pallas kernels for 0%

profile of v1, /device:TPU:6, one launch (start us, length us, event | category | flops | bytes accessed | tf_op | source)
XLA Modules:
  0.0 130.8 jit_solution(7212904270220353236)
XLA Ops:
  7.3 0.9 constant_dynamic-slice_fusion
  8.2 0.1 copy.81
  8.3 0.1 copy.82
  8.4 0.7 pad_maximum_fusion.5
  9.1 0.7 reshape.90
  9.8 1.2 reduce-window.6
  11.0 0.1 slice.49
  11.1 0.1 copy.65
  11.2 0.1 copy.66
  11.3 0.1 add_bitcast_fusion
  11.4 1.1 copy.83
  12.5 0.2 fusion.37
  12.7 0.1 subtract_exponential_fusion
  12.8 1.2 convolution_add_fusion
  14.0 0.1 broadcast_in_dim.98
  14.1 1.9 %collective-permute-start = (f32[4,136,128]{2,1,0:T(8,128)S(1)}, f32[4,136,128]{2,1,0:T(8,128)S(1)}, u32[]{:S(2)}, u32[]{:S(2)}) collective-permute-start(f32[4,136,128]{2,1,0:T(8,128)S(1)} %pad_maximum_fusion), channel_id=1, source_target_pairs={{0,16},{16,32},{32,48},{48,64},{64,80},{80,96},{96,112},{112,128},... | collective-permute-start | bytes 835592 | tf_op jit(solution)/shard_map/ppermute | solution.py:25
  16.0 8.0 %collective-permute-done = f32[4,136,128]{2,1,0:T(8,128)S(1)} collective-permute-done((f32[4,136,128]{2,1,0:T(8,128)S(1)}, f32[4,136,128]{2,1,0:T(8,128)S(1)}, u32[]{:S(2)}, u32[]{:S(2)}) %collective-permute-start) | collective-permute-done | bytes 278560 | tf_op jit(solution)/shard_map/ppermute | solution.py:25
  24.0 0.1 exponential_reduce_fusion.3
  24.2 0.1 multiply_add_fusion.3
  24.3 0.1 broadcast_in_dim.100
  24.4 1.9 %collective-permute-start.1 = (f32[4,136,128]{2,1,0:T(8,128)S(1)}, f32[4,136,128]{2,1,0:T(8,128)S(1)}, u32[]{:S(2)}, u32[]{:S(2)}) collective-permute-start(f32[4,136,128]{2,1,0:T(8,128)S(1)} %pad_maximum_fusion.1), channel_id=1, source_target_pairs={{0,32},{16,48},{32,64},{48,80},{64,96},{80,112},{96,128},{112,144}... | collective-permute-start | bytes 835592 | tf_op jit(solution)/shard_map/ppermute | solution.py:25
  26.3 8.6 %collective-permute-done.1 = f32[4,136,128]{2,1,0:T(8,128)S(1)} collective-permute-done((f32[4,136,128]{2,1,0:T(8,128)S(1)}, f32[4,136,128]{2,1,0:T(8,128)S(1)}, u32[]{:S(2)}, u32[]{:S(2)}) %collective-permute-start.1) | collective-permute-done | bytes 278560 | tf_op jit(solution)/shard_map/ppermute | solution.py:25
  34.9 0.1 exponential_reduce_fusion.2
  35.0 0.1 multiply_add_fusion.2
  35.2 0.1 broadcast_in_dim.102
  35.3 1.9 %collective-permute-start.2 = (f32[4,136,128]{2,1,0:T(8,128)S(1)}, f32[4,136,128]{2,1,0:T(8,128)S(1)}, u32[]{:S(2)}, u32[]{:S(2)}) collective-permute-start(f32[4,136,128]{2,1,0:T(8,128)S(1)} %pad_maximum_fusion.2), channel_id=1, source_target_pairs={{0,64},{16,80},{32,96},{48,112},{64,128},{80,144},{96,160},{112,17... | collective-permute-start | bytes 835592 | tf_op jit(solution)/shard_map/ppermute | solution.py:25
  37.2 9.8 %collective-permute-done.2 = f32[4,136,128]{2,1,0:T(8,128)S(1)} collective-permute-done((f32[4,136,128]{2,1,0:T(8,128)S(1)}, f32[4,136,128]{2,1,0:T(8,128)S(1)}, u32[]{:S(2)}, u32[]{:S(2)}) %collective-permute-start.2) | collective-permute-done | bytes 278560 | tf_op jit(solution)/shard_map/ppermute | solution.py:25
  47.0 0.1 add_reduce_fusion.1
  47.1 0.1 multiply_add_fusion.1
  47.3 0.1 broadcast_in_dim.104
  47.4 1.3 collective-permute-start.3
  48.7 0.7 copy_bitcast_fusion
  49.4 0.7 convolution_bitcast_fusion.1
  50.1 5.7 %collective-permute-done.3 = f32[4,136,128]{2,1,0:T(8,128)S(1)} collective-permute-done((f32[4,136,128]{2,1,0:T(8,128)S(1)}, f32[4,136,128]{2,1,0:T(8,128)S(1)}, u32[]{:S(2)}, u32[]{:S(2)}) %collective-permute-start.3) | collective-permute-done | bytes 278560 | tf_op jit(solution)/shard_map/ppermute | solution.py:25
  55.8 0.1 exponential_reduce_fusion.1
  55.9 0.1 multiply_add_fusion
  56.1 0.1 broadcast_in_dim.106
  56.2 1.3 collective-permute-start.4
  57.5 0.6 fusion.1
  58.1 8.0 %collective-permute-done.4 = f32[4,136,128]{2,1,0:T(8,128)S(1)} collective-permute-done((f32[4,136,128]{2,1,0:T(8,128)S(1)}, f32[4,136,128]{2,1,0:T(8,128)S(1)}, u32[]{:S(2)}, u32[]{:S(2)}) %collective-permute-start.4) | collective-permute-done | bytes 278560 | tf_op jit(solution)/shard_map/ppermute | solution.py:25
  66.1 0.8 multiply_reduce_fusion
  66.9 0.2 copy.76
  67.1 4.9 %psum.28 = f32[256]{0:T(256)S(1)} all-reduce(f32[256]{0:T(256)S(1)} %get-tuple-element.51), channel_id=1, replica_groups=mesh['ctx'=32,'head_8'=2,'head_4'=2,'head_2'=2,'head_1'=2] {'head_1'}, use_global_device_ids=true, to_apply=%region_3.4 | all-reduce | flops 256 | bytes 2048 | tf_op jit(solution)/shard_map/psum | solution.py:81
  72.1 5.8 %psum.29 = f32[256]{0:T(256)S(1)} all-reduce(f32[256]{0:T(256)S(1)} %psum.28), channel_id=1, replica_groups=mesh['ctx'=32,'head_8'=2,'head_4'=2,'head_2'=2,'head_1'=2] {'head_2'}, use_global_device_ids=true, to_apply=%region_4.5 | all-reduce | flops 256 | bytes 2048 | tf_op jit(solution)/shard_map/psum | solution.py:81
  77.9 9.6 %psum.30 = f32[256]{0:T(256)S(1)} all-reduce(f32[256]{0:T(256)S(1)} %psum.29), channel_id=1, replica_groups=mesh['ctx'=32,'head_8'=2,'head_4'=2,'head_2'=2,'head_1'=2] {'head_4'}, use_global_device_ids=true, to_apply=%region_5.6 | all-reduce | flops 256 | bytes 2048 | tf_op jit(solution)/shard_map/psum | solution.py:81
  87.5 17.0 %psum.31 = f32[256]{0:T(256)S(1)} all-reduce(f32[256]{0:T(256)S(1)} %psum.30), channel_id=1, replica_groups=mesh['ctx'=32,'head_8'=2,'head_4'=2,'head_2'=2,'head_1'=2] {'head_8'}, use_global_device_ids=true, to_apply=%region_6.7 | all-reduce | flops 256 | bytes 2048 | tf_op jit(solution)/shard_map/psum | solution.py:81
  104.5 0.8 multiply_convert_fusion
  105.3 18.6 %shard_map.95 = bf16[256,512]{1,0:T(8,128)(2,1)} custom-call(s32[1]{0:T(128)} %bitcast.11.index_ref, bf16[1024,128]{1,0:T(8,128)(2,1)} %bitcast.84, bf16[256,8192]{1,0:T(8,128)(2,1)} %bitcast.82), custom_call_target="tpu_custom_call" | custom-call | tf_op jit(solution)/shard_map/pallas_call | solution.py:145
  (22 shorter events, 0.3 us)
Async XLA Ops:
  7.2 42.2 %copy-start = (bf16[256,512]{1,0:T(8,128)(2,1)S(1)}, bf16[256,512]{1,0:T(8,128)(2,1)}, u32[]{:S(2)}) copy-start(bf16[256,512]{1,0:T(8,128)(2,1)} %param.8) | copy-start | bytes 786436
  7.2 41.5 %copy-start.1 = (bf16[256,512]{1,0:T(8,128)(2,1)S(1)}, bf16[256,512]{1,0:T(8,128)(2,1)}, u32[]{:S(2)}) copy-start(bf16[256,512]{1,0:T(8,128)(2,1)} %param.13) | copy-start | bytes 786436
  7.2 98.1 %all-gather.2.cloned.1.call-start = ((), (), s32[]{:S(2)}) async-start(), calls=%async_computation | async-start | bytes 4325376 | tf_op jit(solution)/shard_map/all_gather | solution.py:171
  14.1 10.0 %collective-permute-start = (f32[4,136,128]{2,1,0:T(8,128)S(1)}, f32[4,136,128]{2,1,0:T(8,128)S(1)}, u32[]{:S(2)}, u32[]{:S(2)}) collective-permute-start(f32[4,136,128]{2,1,0:T(8,128)S(1)} %pad_maximum_fusion), channel_id=1, source_target_pairs={{0,16},{16,32},{32,48},{48,64},{64,80},{80,96},{96,112},{112,128},... | collective-permute-start | bytes 835592 | tf_op jit(solution)/shard_map/ppermute | solution.py:25
  24.2 33.3 %copy-start.2 = (bf16[256,512]{1,0:T(8,128)(2,1)S(1)}, bf16[256,512]{1,0:T(8,128)(2,1)}, u32[]{:S(2)}) copy-start(bf16[256,512]{1,0:T(8,128)(2,1)} %param.10) | copy-start | bytes 786436
  24.4 10.6 %collective-permute-start.1 = (f32[4,136,128]{2,1,0:T(8,128)S(1)}, f32[4,136,128]{2,1,0:T(8,128)S(1)}, u32[]{:S(2)}, u32[]{:S(2)}) collective-permute-start(f32[4,136,128]{2,1,0:T(8,128)S(1)} %pad_maximum_fusion.1), channel_id=1, source_target_pairs={{0,32},{16,48},{32,64},{48,80},{64,96},{80,112},{96,128},{112,144}... | collective-permute-start | bytes 835592 | tf_op jit(solution)/shard_map/ppermute | solution.py:25
  35.3 11.8 %collective-permute-start.2 = (f32[4,136,128]{2,1,0:T(8,128)S(1)}, f32[4,136,128]{2,1,0:T(8,128)S(1)}, u32[]{:S(2)}, u32[]{:S(2)}) collective-permute-start(f32[4,136,128]{2,1,0:T(8,128)S(1)} %pad_maximum_fusion.2), channel_id=1, source_target_pairs={{0,64},{16,80},{32,96},{48,112},{64,128},{80,144},{96,160},{112,17... | collective-permute-start | bytes 835592 | tf_op jit(solution)/shard_map/ppermute | solution.py:25
  47.4 8.4 %collective-permute-start.3 = (f32[4,136,128]{2,1,0:T(8,128)S(1)}, f32[4,136,128]{2,1,0:T(8,128)S(1)}, u32[]{:S(2)}, u32[]{:S(2)}) collective-permute-start(f32[4,136,128]{2,1,0:T(8,128)S(1)} %pad_maximum_fusion.3), channel_id=1, source_target_pairs={{0,128},{16,144},{32,160},{48,176},{64,192},{80,208},{96,224},{112... | collective-permute-start | bytes 835592 | tf_op jit(solution)/shard_map/ppermute | solution.py:25
  49.4 55.1 %copy-start.3 = (f32[512]{0:T(512)S(1)}, f32[512]{0:T(512)}, u32[]{:S(2)}) copy-start(f32[512]{0:T(512)} %param.12) | copy-start | bytes 6148
  56.2 9.9 %collective-permute-start.4 = (f32[4,136,128]{2,1,0:T(8,128)S(1)}, f32[4,136,128]{2,1,0:T(8,128)S(1)}, u32[]{:S(2)}, u32[]{:S(2)}) collective-permute-start(f32[4,136,128]{2,1,0:T(8,128)S(1)} %pad_maximum_fusion.4), channel_id=1, source_target_pairs={{0,256},{16,272},{32,288},{48,304},{64,320},{80,336},{96,352},{112... | collective-permute-start | bytes 835592 | tf_op jit(solution)/shard_map/ppermute | solution.py:25
Sparse Core Ops, SparseCore 0:
  11.6 72.3 all-gather.1

commit v2 on v0

--- a/solution.py
+++ b/solution.py
@@ -86,25 +86,27 @@
     row_count = o_ref.shape[0]
     head_count = o_ref.shape[1] // DH
     wide = q_ref.shape[0]
+    held = kvt_ref.shape[1]
     max_ref[...] = jnp.full(max_ref.shape, NEGATIVE, jnp.float32)
     total_ref[...] = jnp.zeros(total_ref.shape, jnp.float32)
     acc_ref[...] = jnp.zeros(acc_ref.shape, jnp.float32)
-    full_blocks = (my_index * row_count) // KEY_BLOCK
-    block_count = (my_index * row_count + row_count - 1) // KEY_BLOCK + 1
+    needed = (my_index + 1) * row_count
+    offset = needed - held
+    block_count = (needed + KEY_BLOCK - 1) // KEY_BLOCK
 
     def update(block, masked):
-        start = pl.multiple_of(block * KEY_BLOCK, KEY_BLOCK)
+        start = pl.multiple_of(held - (block_count - block) * KEY_BLOCK, KEY_BLOCK)
         keys_t = kvt_ref[0:DH, pl.ds(start, KEY_BLOCK)]
         values_t = kvt_ref[DH : 2 * DH, pl.ds(start, KEY_BLOCK)]
         scores = lax.dot_general(
             keys_t, q_ref[...], (((0,), (1,)), ((), ())), preferred_element_type=jnp.float32
         ) * DH ** (-0.5)
         if masked:
-            key_pos = start + lax.broadcasted_iota(jnp.int32, (KEY_BLOCK, wide), 0)
+            key_pos = start + offset + lax.broadcasted_iota(jnp.int32, (KEY_BLOCK, wide), 0)
             query_pos = my_index * row_count + lax.rem(
                 lax.broadcasted_iota(jnp.int32, (KEY_BLOCK, wide), 1), row_count
             )
-            allowed = key_pos <= query_pos
+            allowed = jnp.logical_and(key_pos >= 0, key_pos <= query_pos)
             scores = jnp.where(allowed, scores, NEGATIVE)
         row_max = max_ref[...]
         new_max = jnp.maximum(row_max, jnp.max(scores, axis=0, keepdims=True))
@@ -123,24 +125,24 @@
         update(block, False)
         return carry
 
-    def diagonal(block, carry):
-        update(block, True)
-        return carry
-
-    lax.fori_loop(0, full_blocks, plain, 0)
-    lax.fori_loop(full_blocks, block_count, diagonal, 0)
+    update(0, True)
+    lax.fori_loop(1, block_count - 1, plain, 0)
+
+    @pl.when(block_count > 1)
+    def _():
+        update(block_count - 1, True)
+
     for head in range(head_count):
         cols = slice(head * row_count, (head + 1) * row_count)
         ratio = acc_ref[:, cols] / total_ref[:, cols]
         o_ref[:, head * DH : (head + 1) * DH] = ratio.T.astype(o_ref.dtype)
 
 
-def soft_attention(my_index, queries, keys_values):
+def soft_attention(my_index, queries, keys_values_t):
     row_count, width = queries.shape
     head_count = width // DH
     wide = head_count * row_count
     stacked = queries.reshape(row_count, head_count, DH).transpose(1, 0, 2).reshape(wide, DH)
-    keys_values_t = keys_values.T
     return pl.pallas_call(
         soft_kernel,
         out_shape=jax.ShapeDtypeStruct((row_count, width), jnp.bfloat16),
@@ -158,6 +160,16 @@
     )(my_index.reshape(1), stacked, keys_values_t)
 
 
+def prefix_window(block, axis):
+    window = block
+    count = lax.axis_size(axis)
+    step = 1
+    while step < count:
+        window = jnp.concatenate([shifted(window, axis, step), window], axis=1)
+        step *= 2
+    return window
+
+
 def layer(q_linear, k_linear, v_linear, log_decay, norm_gain, q_soft, k_soft, v_soft):
     row_count = q_linear.shape[0]
     head_count = log_decay.shape[1]
@@ -167,9 +179,7 @@
     kv_start = lax.axis_index(HEAD_AXES) * head_count // group_size
     k_local = lax.dynamic_slice_in_dim(k_soft, kv_start * DH, kv_count * DH, 1)
     v_local = lax.dynamic_slice_in_dim(v_soft, kv_start * DH, kv_count * DH, 1)
-    keys_values = lax.all_gather(
-        jnp.concatenate([k_local, v_local], axis=1), "ctx", axis=0, tiled=True
-    )
+    keys_values_t = prefix_window(jnp.concatenate([k_local, v_local], axis=1).T, "ctx")
 
     local_blocks = row_count // BLOCK
     lin_shape = (local_blocks, BLOCK, head_count, DH)
@@ -198,7 +208,7 @@
 
     my_index = lax.axis_index("ctx").astype(jnp.int32)
     if kv_count == 1:
-        soft_out = soft_attention(my_index, q_soft, keys_values)
+        soft_out = soft_attention(my_index, q_soft, keys_values_t)
     else:
         raise NotImplementedError("kv_count > 1")
     return (linear_out, soft_out)

time: 128 us -> 201 us (1.57)
  waiting for transfers between devices: 40.4 us -> 102 us
  between operations: 14.3 us -> 0.96 us
  starting transfers between devices: 8.38 us -> 19.5 us
  local copies, waits for them, and re-layouts: 4.7 us -> 14.7 us
  matrix products: 3.28 us -> 6.17 us
  blocking collectives: 33.6 us -> 31.5 us
  other arithmetic: 3.97 us -> 6.04 us
    ppermute x5 -> x10, waiting for transfers between devices: 40.4 us -> 102 us  [shifted(): lax.ppermute(value, axis, [(source, source + steps) for source in range(f...]
    ppermute x5 -> x10, starting transfers between devices: 8.35 us -> 19.5 us  [shifted(): lax.ppermute(value, axis, [(source, source + steps) for source in range(f...]
    unnamed x11 -> x28, local copies, waits for them, and re-layouts: 0.24 us -> 10.2 us
    psum x1, blocking collectives: 21.3 us -> 18.5 us  [split_sum(): return lax.psum(partial, 'head_hi')]
  transfers between devices with their start and end apart: 6 -> 10, of which waited for: 5 -> 7; matrix products, arithmetic and copies ran while one was open for 8% -> 7% of each run, Pallas kernels for 0% -> 0%
where the time goes in v2:
time: 201 us; the launch traced here: 200 us
  waiting for transfers between devices  102 us (51%)
  blocking collectives  31.5 us (16%)
  starting transfers between devices  19.5 us (10%)
  Pallas kernels  19.4 us (10%)
  local copies, waits for them, and re-layouts  14.7 us (7%)
  matrix products  6.17 us (3%)
  other arithmetic  6.04 us (3%)
    ppermute x10, waiting for transfers between devices, shifted(): lax.ppermute(value, axis, [(source, source + steps) for source in range(f...  102 us
    ppermute x10, starting transfers between devices, shifted(): lax.ppermute(value, axis, [(source, source + steps) for source in range(f...  19.5 us
    pallas_call x1, Pallas kernels, soft_attention(): pl.pallas_call(soft_kernel, out_shape=jax.ShapeDtypeStruct((row_count, wi...  19.4 us
    psum x1, blocking collectives, split_sum(): return lax.psum(partial, 'head_hi')  18.5 us
    psum x1, blocking collectives, split_sum(): partial = lax.optimization_barrier(lax.psum(value, 'head_lo'))  13 us
    unnamed x28, local copies, waits for them, and re-layouts  10.2 us
  transfers between devices with their start and end apart: 10, of which 7 were waited for; matrix products, arithmetic and copies ran while one was open for 7% of the time, Pallas kernels for 0%

profile of v2, /device:TPU:6, one launch (start us, length us, event | category | flops | bytes accessed | tf_op | source)
XLA Modules:
  0.0 200.5 jit_solution(1802148861159463802)
XLA Ops:
  0.6 0.7 reshape.90
  1.4 1.2 reduce-window.6
  3.0 0.2 fusion.37
  3.3 1.1 copy.83
  4.4 1.2 convolution_add_fusion
  5.6 1.9 collective-permute-start
  7.6 0.9 constant_dynamic-slice_fusion
  8.7 3.6 %collective-permute-start.5 = (bf16[256,256]{1,0:T(8,128)(2,1)S(1)}, bf16[256,256]{1,0:T(8,128)(2,1)S(1)}, u32[]{:S(2)}, u32[]{:S(2)}) collective-permute-start(bf16[256,256]{1,0:T(8,128)(2,1)S(1)} %maximum_bitcast_fusion), channel_id=1, source_target_pairs={{0,16},{16,32},{32,48},{48,64},{64,80},{80,96},{96,112},{112,128},... | collective-permute-start | bytes 393224 | tf_op jit(solution)/shard_map/ppermute | solution.py:25
  12.3 4.8 %collective-permute-done.5 = bf16[256,256]{1,0:T(8,128)(2,1)S(1)} collective-permute-done((bf16[256,256]{1,0:T(8,128)(2,1)S(1)}, bf16[256,256]{1,0:T(8,128)(2,1)S(1)}, u32[]{:S(2)}, u32[]{:S(2)}) %collective-permute-start.5) | collective-permute-done | bytes 131104 | tf_op jit(solution)/shard_map/ppermute | solution.py:25
  17.2 1.9 collective-permute-start.6
  19.2 0.1 exponential_reduce_fusion.3
  19.4 2.9 %collective-permute-start.1 = (f32[4,136,128]{2,1,0:T(8,128)S(1)}, f32[4,136,128]{2,1,0:T(8,128)S(1)}, u32[]{:S(2)}, u32[]{:S(2)}) collective-permute-start(f32[4,136,128]{2,1,0:T(8,128)S(1)} %pad_maximum_fusion.3), channel_id=1, source_target_pairs={{0,32},{16,48},{32,64},{48,80},{64,96},{80,112},{96,128},{112,144}... | collective-permute-start | bytes 835592 | tf_op jit(solution)/shard_map/ppermute | solution.py:25
  22.4 8.0 %collective-permute-done.6 = bf16[256,512]{1,0:T(8,128)(2,1)S(1)} collective-permute-done((bf16[256,512]{1,0:T(8,128)(2,1)S(1)}, bf16[256,512]{1,0:T(8,128)(2,1)S(1)}, u32[]{:S(2)}, u32[]{:S(2)}) %collective-permute-start.6) | collective-permute-done | bytes 262176 | tf_op jit(solution)/shard_map/ppermute | solution.py:25
  30.4 1.9 collective-permute-start.7
  32.3 5.3 %collective-permute-done.1 = f32[4,136,128]{2,1,0:T(8,128)S(1)} collective-permute-done((f32[4,136,128]{2,1,0:T(8,128)S(1)}, f32[4,136,128]{2,1,0:T(8,128)S(1)}, u32[]{:S(2)}, u32[]{:S(2)}) %collective-permute-start.1) | collective-permute-done | bytes 278560 | tf_op jit(solution)/shard_map/ppermute | solution.py:25
  37.8 6.9 %collective-permute-done.7 = bf16[256,1024]{1,0:T(8,128)(2,1)S(1)} collective-permute-done((bf16[256,1024]{1,0:T(8,128)(2,1)S(1)}, bf16[256,1024]{1,0:T(8,128)(2,1)S(1)}, u32[]{:S(2)}, u32[]{:S(2)}) %collective-permute-start.7) | collective-permute-done | bytes 524320 | tf_op jit(solution)/shard_map/ppermute | solution.py:25
  44.8 1.3 collective-permute-start.8
  46.1 0.1 exponential_reduce_fusion.2
  46.3 1.9 collective-permute-start.2
  48.2 27.0 %collective-permute-done.2 = f32[4,136,128]{2,1,0:T(8,128)S(1)} collective-permute-done((f32[4,136,128]{2,1,0:T(8,128)S(1)}, f32[4,136,128]{2,1,0:T(8,128)S(1)}, u32[]{:S(2)}, u32[]{:S(2)}) %collective-permute-start.2) | collective-permute-done | bytes 278560 | tf_op jit(solution)/shard_map/ppermute | solution.py:25
  75.6 1.4 collective-permute-start.3
  77.0 1.0 constant_dynamic-update-slice_fusion.4
  78.0 0.9 constant_dynamic-update-slice_fusion.3
  78.9 0.8 constant_dynamic-update-slice_fusion.2
  79.7 0.7 constant_dynamic-update-slice_fusion.1
  80.4 0.7 constant_dynamic-update-slice_fusion
  81.1 1.3 collective-permute-start.9
  82.4 0.8 copy_bitcast_fusion
  83.1 0.7 convolution_bitcast_fusion.1
  83.9 0.3 collective-permute-done.3
  84.2 0.6 exponential_reduce_fusion.1
  84.8 0.1 multiply_add_fusion
  85.0 0.7 pad_maximum_fusion.6
  85.7 1.3 collective-permute-start.4
  87.1 2.3 %fusion.1 = f32[256,4,128]{0,2,1:T(8,128)} fusion(f32[256,4,128]{0,2,1:T(8,128)S(1)} %convolution_bitcast_fusion.1, bf16[256,4,128]{0,2,1:T(8,128)(2,1)S(1)} %bitcast.90, f32[4,256]{1,0:T(4,128)S(1)} %bitcast.96, pred[256,256]{1,0:T(8,128)(4,1)S(1)} %iota_compare_fusion, bf16[256,512]{1,0:T(8,128)(2,1)} %param.10, bf16[256,512]{1,0:T(8,128)(2,1)S(1)} %copy-done), kind=kOutput, calls=%fused_computation.5 | convolution fusion | flops 135397376 | bytes 1904640 | tf_op jit(solution)/shard_map/while/body/eval_jaxpr/hts,she->the/dot_general | solution.py:40
  89.4 49.9 %collective-permute-done.4 = f32[4,136,128]{2,1,0:T(8,128)} collective-permute-done((f32[4,136,128]{2,1,0:T(8,128)}, f32[4,136,128]{2,1,0:T(8,128)}, u32[]{:S(2)}, u32[]{:S(2)}) %collective-permute-start.4) | collective-permute-done | bytes 278560 | tf_op jit(solution)/shard_map/ppermute | solution.py:25
  139.3 2.0 multiply_reduce_fusion
  141.3 0.2 copy.76
  141.5 13.0 %psum.14 = f32[256]{0:T(256)S(1)} all-reduce(f32[256]{0:T(256)S(1)} %get-tuple-element.51), channel_id=1, replica_groups=mesh['ctx'=32,'head_hi'=4,'head_lo'=4] {'head_lo'}, use_global_device_ids=true, to_apply=%region_3.4 | all-reduce | flops 256 | bytes 2048 | tf_op jit(solution)/shard_map/psum | solution.py:80
  154.5 18.5 %psum.15 = f32[256]{0:T(256)S(1)} all-reduce(f32[256]{0:T(256)S(1)} %psum.14), channel_id=1, replica_groups=mesh['ctx'=32,'head_hi'=4,'head_lo'=4] {'head_hi'}, use_global_device_ids=true, to_apply=%region_4.5 | all-reduce | flops 256 | bytes 2048 | tf_op jit(solution)/shard_map/psum | solution.py:81
  173.1 0.8 multiply_convert_fusion
  173.9 3.2 %constant_dynamic-update-slice_fusion.10 = bf16[256,8192]{1,0:T(8,128)(2,1)} fusion(bf16[256,4096]{1,0:T(8,128)(2,1)} %collective-permute-done.9), kind=kLoop, calls=%fused_computation.67 | loop fusion | bytes 4194304
  177.1 1.1 constant_dynamic-update-slice_fusion.9
  178.1 0.9 constant_dynamic-update-slice_fusion.8
  179.0 0.7 constant_dynamic-update-slice_fusion.7
  179.7 0.7 constant_dynamic-update-slice_fusion.6
  180.5 0.7 constant_dynamic-update-slice_fusion.5.kvt_ref
  181.1 19.4 %shard_map.95 = bf16[256,512]{1,0:T(8,128)(2,1)} custom-call(s32[1]{0:T(128)} %bitcast.11.index_ref, bf16[1024,128]{1,0:T(8,128)(2,1)} %bitcast.88, bf16[256,8192]{1,0:T(8,128)(2,1)} %constant_dynamic-update-slice_fusion.5.kvt_ref), custom_call_target="tpu_custom_call" | custom-call | tf_op jit(solution)/shard_map/pallas_call | solution.py:146
  (49 shorter events, 1.8 us)
Async XLA Ops:
  0.6 82.5 %copy-start = (bf16[256,512]{1,0:T(8,128)(2,1)S(1)}, bf16[256,512]{1,0:T(8,128)(2,1)}, u32[]{:S(2)}) copy-start(bf16[256,512]{1,0:T(8,128)(2,1)} %param.8) | copy-start | bytes 786436
  5.6 13.5 %collective-permute-start = (f32[4,136,128]{2,1,0:T(8,128)S(1)}, f32[4,136,128]{2,1,0:T(8,128)S(1)}, u32[]{:S(2)}, u32[]{:S(2)}) collective-permute-start(f32[4,136,128]{2,1,0:T(8,128)S(1)} %pad_maximum_fusion.2), channel_id=1, source_target_pairs={{0,16},{16,32},{32,48},{48,64},{64,80},{80,96},{96,112},{112,128},... | collective-permute-start | bytes 835592 | tf_op jit(solution)/shard_map/ppermute | solution.py:25
  8.6 71.8 %copy-start.1 = (bf16[256,128]{0,1:T(8,128)(2,1)}, bf16[256,128]{0,1:T(8,128)(2,1)S(1)}, u32[]{:S(2)}) copy-start(bf16[256,128]{0,1:T(8,128)(2,1)S(1)} %copy.81) | copy-start | bytes 196612
  8.7 71.7 %copy-start.3 = (bf16[256,128]{0,1:T(8,128)(2,1)}, bf16[256,128]{0,1:T(8,128)(2,1)S(1)}, u32[]{:S(2)}) copy-start(bf16[256,128]{0,1:T(8,128)(2,1)S(1)} %copy.82) | copy-start | bytes 196612
  8.7 8.4 %collective-permute-start.5 = (bf16[256,256]{1,0:T(8,128)(2,1)S(1)}, bf16[256,256]{1,0:T(8,128)(2,1)S(1)}, u32[]{:S(2)}, u32[]{:S(2)}) collective-permute-start(bf16[256,256]{1,0:T(8,128)(2,1)S(1)} %maximum_bitcast_fusion), channel_id=1, source_target_pairs={{0,16},{16,32},{32,48},{48,64},{64,80},{80,96},{96,112},{112,128},... | collective-permute-start | bytes 393224 | tf_op jit(solution)/shard_map/ppermute | solution.py:25
  17.2 13.2 %collective-permute-start.6 = (bf16[256,512]{1,0:T(8,128)(2,1)S(1)}, bf16[256,512]{1,0:T(8,128)(2,1)S(1)}, u32[]{:S(2)}, u32[]{:S(2)}) collective-permute-start(bf16[256,512]{1,0:T(8,128)(2,1)S(1)} %pad_maximum_fusion.7), channel_id=1, source_target_pairs={{0,32},{16,48},{32,64},{48,80},{64,96},{80,112},{96,128},{112,144}... | collective-permute-start | bytes 786440 | tf_op jit(solution)/shard_map/ppermute | solution.py:25
  19.4 18.2 %collective-permute-start.1 = (f32[4,136,128]{2,1,0:T(8,128)S(1)}, f32[4,136,128]{2,1,0:T(8,128)S(1)}, u32[]{:S(2)}, u32[]{:S(2)}) collective-permute-start(f32[4,136,128]{2,1,0:T(8,128)S(1)} %pad_maximum_fusion.3), channel_id=1, source_target_pairs={{0,32},{16,48},{32,64},{48,80},{64,96},{80,112},{96,128},{112,144}... | collective-permute-start | bytes 835592 | tf_op jit(solution)/shard_map/ppermute | solution.py:25
  30.4 14.3 %collective-permute-start.7 = (bf16[256,1024]{1,0:T(8,128)(2,1)S(1)}, bf16[256,1024]{1,0:T(8,128)(2,1)S(1)}, u32[]{:S(2)}, u32[]{:S(2)}) collective-permute-start(bf16[256,1024]{1,0:T(8,128)(2,1)S(1)} %pad_maximum_fusion.1), channel_id=1, source_target_pairs={{0,64},{16,80},{32,96},{48,112},{64,128},{80,144},{96,160},{112,17... | collective-permute-start | bytes 1572872 | tf_op jit(solution)/shard_map/ppermute | solution.py:25
  44.8 32.2 %collective-permute-start.8 = (bf16[256,2048]{1,0:T(8,128)(2,1)S(1)}, bf16[256,2048]{1,0:T(8,128)(2,1)S(1)}, u32[]{:S(2)}, u32[]{:S(2)}) collective-permute-start(bf16[256,2048]{1,0:T(8,128)(2,1)S(1)} %pad_maximum_fusion), channel_id=1, source_target_pairs={{0,128},{16,144},{32,160},{48,176},{64,192},{80,208},{96,224},{112... | collective-permute-start | bytes 3145736 | tf_op jit(solution)/shard_map/ppermute | solution.py:25
  46.3 28.9 %collective-permute-start.2 = (f32[4,136,128]{2,1,0:T(8,128)S(1)}, f32[4,136,128]{2,1,0:T(8,128)S(1)}, u32[]{:S(2)}, u32[]{:S(2)}) collective-permute-start(f32[4,136,128]{2,1,0:T(8,128)S(1)} %pad_maximum_fusion.4), channel_id=1, source_target_pairs={{0,64},{16,80},{32,96},{48,112},{64,128},{80,144},{96,160},{112,17... | collective-permute-start | bytes 835592 | tf_op jit(solution)/shard_map/ppermute | solution.py:25
  75.6 6.8 %copy-start.5 = (bf16[256,512]{1,0:T(8,128)(2,1)S(1)}, bf16[256,512]{1,0:T(8,128)(2,1)}, u32[]{:S(2)}) copy-start(bf16[256,512]{1,0:T(8,128)(2,1)} %param.13) | copy-start | bytes 786436
  75.6 8.6 %collective-permute-start.3 = (f32[4,136,128]{2,1,0:T(8,128)S(1)}, f32[4,136,128]{2,1,0:T(8,128)S(1)}, u32[]{:S(2)}, u32[]{:S(2)}) collective-permute-start(f32[4,136,128]{2,1,0:T(8,128)S(1)} %pad_maximum_fusion.5), channel_id=1, source_target_pairs={{0,128},{16,144},{32,160},{48,176},{64,192},{80,208},{96,224},{112... | collective-permute-start | bytes 835592 | tf_op jit(solution)/shard_map/ppermute | solution.py:25
  81.1 92.8 %collective-permute-start.9 = (bf16[256,4096]{1,0:T(8,128)(2,1)}, bf16[256,4096]{1,0:T(8,128)(2,1)}, u32[]{:S(2)}, u32[]{:S(2)}) collective-permute-start(bf16[256,4096]{1,0:T(8,128)(2,1)} %constant_dynamic-update-slice_fusion), channel_id=1, source_target_pairs={{0,256},{16,272},{32,288},{48,304},{64,320},{80,336},{96,352},{112... | collective-permute-start | bytes 6291464 | tf_op jit(solution)/shard_map/ppermute | solution.py:25
  84.9 54.4 %copy-start.7 = (f32[4]{0:T(128)S(1)}, f32[4]{0:T(128)}, u32[]{:S(2)}) copy-start(f32[4]{0:T(128)} %get-tuple-element.20) | copy-start | bytes 52
  85.7 53.6 %collective-permute-start.4 = (f32[4,136,128]{2,1,0:T(8,128)}, f32[4,136,128]{2,1,0:T(8,128)}, u32[]{:S(2)}, u32[]{:S(2)}) collective-permute-start(f32[4,136,128]{2,1,0:T(8,128)} %pad_maximum_fusion.6), channel_id=1, source_target_pairs={{0,256},{16,272},{32,288},{48,304},{64,320},{80,336},{96,352},{112... | collective-permute-start | bytes 835592 | tf_op jit(solution)/shard_map/ppermute | solution.py:25
  89.4 83.7 %copy-start.6 = (f32[512]{0:T(512)S(1)}, f32[512]{0:T(512)}, u32[]{:S(2)}) copy-start(f32[512]{0:T(512)} %param.12) | copy-start | bytes 6148
  177.0 3.4 %copy-start.2 = (bf16[256,128]{0,1:T(8,128)(2,1)S(1)}, bf16[256,128]{0,1:T(8,128)(2,1)}, u32[]{:S(2)}) copy-start(bf16[256,128]{0,1:T(8,128)(2,1)} %copy-done.1) | copy-start | bytes 196612
  177.1 3.4 %copy-start.4 = (bf16[256,128]{0,1:T(8,128)(2,1)S(1)}, bf16[256,128]{0,1:T(8,128)(2,1)}, u32[]{:S(2)}) copy-start(bf16[256,128]{0,1:T(8,128)(2,1)} %copy-done.3) | copy-start | bytes 196612

commit v3 on v1

--- a/solution.py
+++ b/solution.py
@@ -12,7 +12,7 @@
 KV_HEADS = 8
 BLOCK = 256
 KEY_BLOCK = 512
-HEAD_AXES = ("head_8", "head_4", "head_2", "head_1")
+HEAD_AXES = ("head_hi", "head_2", "head_1")
 
 
 EPSILON = 1e-06
@@ -207,9 +207,8 @@
 
 def solution(mesh):
     ctx_count, head_count = mesh.devices.shape
-    assert head_count == 2 ** len(HEAD_AXES)
     split = jax.sharding.Mesh(
-        np.asarray(mesh.devices).reshape((ctx_count,) + (2,) * len(HEAD_AXES)), ("ctx",) + HEAD_AXES
+        np.asarray(mesh.devices).reshape(ctx_count, head_count // 4, 2, 2), ("ctx",) + HEAD_AXES
     )
     return jax.shard_map(
         layer,

time: 131 us -> 128 us (0.977)
  blocking collectives: 37.4 us -> 34.3 us
    psum x4 -> x3, blocking collectives: 37.4 us -> 34.3 us  [split_sum(): value = lax.psum(value, axis)]
where the time goes in v3:
time: 128 us
  waiting for transfers between devices  40.4 us (32%)
  blocking collectives  34.3 us (27%)
  Pallas kernels  18.6 us (15%)
  between operations  14.3 us (11%)
  starting transfers between devices  8.38 us (7%)
  local copies, waits for them, and re-layouts  4.7 us (4%)
  other arithmetic  3.97 us (3%)
  matrix products  3.28 us (3%)
    ppermute x5, waiting for transfers between devices, shifted(): lax.ppermute(value, axis, [(source, source + steps) for source in range(f...  40.4 us
    psum x3, blocking collectives, split_sum(): value = lax.psum(value, axis)  34.3 us
    pallas_call x1, Pallas kernels, soft_attention(): pl.pallas_call(soft_kernel, out_shape=jax.ShapeDtypeStruct((row_count, wi...  18.6 us
    ppermute x5, starting transfers between devices, shifted(): lax.ppermute(value, axis, [(source, source + steps) for source in range(f...  8.35 us
  transfers between devices with their start and end apart: 6, of which 5 were waited for; matrix products, arithmetic and copies ran while one was open for 8% of the time, Pallas kernels for 0%

profile of v3, /device:TPU:6, one launch (start us, length us, event | category | flops | bytes accessed | tf_op | source)
XLA Modules:
  0.0 128.0 jit_solution(16488709277274126921)
XLA Ops:
  7.2 0.0 all-gather.2.cloned.1.call-start
  7.3 0.9 constant_dynamic-slice_fusion
  8.2 0.1 copy.81
  8.3 0.1 copy.82
  8.4 0.7 pad_maximum_fusion.5
  9.1 0.7 reshape.90
  9.8 1.2 reduce-window.6
  11.0 0.1 slice.49
  11.1 0.1 copy.65
  11.2 0.1 copy.66
  11.3 0.1 add_bitcast_fusion
  11.4 1.1 copy.83
  12.5 0.2 fusion.37
  12.7 0.1 subtract_exponential_fusion
  12.8 1.2 convolution_add_fusion
  14.0 0.1 broadcast_in_dim.98
  14.1 1.9 %collective-permute-start = (f32[4,136,128]{2,1,0:T(8,128)S(1)}, f32[4,136,128]{2,1,0:T(8,128)S(1)}, u32[]{:S(2)}, u32[]{:S(2)}) collective-permute-start(f32[4,136,128]{2,1,0:T(8,128)S(1)} %pad_maximum_fusion), channel_id=1, source_target_pairs={{0,16},{16,32},{32,48},{48,64},{64,80},{80,96},{96,112},{112,128},... | collective-permute-start | bytes 835592 | tf_op jit(solution)/shard_map/ppermute | solution.py:25
  16.0 8.0 %collective-permute-done = f32[4,136,128]{2,1,0:T(8,128)S(1)} collective-permute-done((f32[4,136,128]{2,1,0:T(8,128)S(1)}, f32[4,136,128]{2,1,0:T(8,128)S(1)}, u32[]{:S(2)}, u32[]{:S(2)}) %collective-permute-start) | collective-permute-done | bytes 278560 | tf_op jit(solution)/shard_map/ppermute | solution.py:25
  24.0 0.1 exponential_reduce_fusion.3
  24.2 0.1 multiply_add_fusion.3
  24.3 0.1 broadcast_in_dim.100
  24.4 1.9 %collective-permute-start.1 = (f32[4,136,128]{2,1,0:T(8,128)S(1)}, f32[4,136,128]{2,1,0:T(8,128)S(1)}, u32[]{:S(2)}, u32[]{:S(2)}) collective-permute-start(f32[4,136,128]{2,1,0:T(8,128)S(1)} %pad_maximum_fusion.1), channel_id=1, source_target_pairs={{0,32},{16,48},{32,64},{48,80},{64,96},{80,112},{96,128},{112,144}... | collective-permute-start | bytes 835592 | tf_op jit(solution)/shard_map/ppermute | solution.py:25
  26.3 8.6 %collective-permute-done.1 = f32[4,136,128]{2,1,0:T(8,128)S(1)} collective-permute-done((f32[4,136,128]{2,1,0:T(8,128)S(1)}, f32[4,136,128]{2,1,0:T(8,128)S(1)}, u32[]{:S(2)}, u32[]{:S(2)}) %collective-permute-start.1) | collective-permute-done | bytes 278560 | tf_op jit(solution)/shard_map/ppermute | solution.py:25
  34.9 0.1 exponential_reduce_fusion.2
  35.0 0.1 multiply_add_fusion.2
  35.2 0.1 broadcast_in_dim.102
  35.3 1.9 %collective-permute-start.2 = (f32[4,136,128]{2,1,0:T(8,128)S(1)}, f32[4,136,128]{2,1,0:T(8,128)S(1)}, u32[]{:S(2)}, u32[]{:S(2)}) collective-permute-start(f32[4,136,128]{2,1,0:T(8,128)S(1)} %pad_maximum_fusion.2), channel_id=1, source_target_pairs={{0,64},{16,80},{32,96},{48,112},{64,128},{80,144},{96,160},{112,17... | collective-permute-start | bytes 835592 | tf_op jit(solution)/shard_map/ppermute | solution.py:25
  37.2 10.0 %collective-permute-done.2 = f32[4,136,128]{2,1,0:T(8,128)S(1)} collective-permute-done((f32[4,136,128]{2,1,0:T(8,128)S(1)}, f32[4,136,128]{2,1,0:T(8,128)S(1)}, u32[]{:S(2)}, u32[]{:S(2)}) %collective-permute-start.2) | collective-permute-done | bytes 278560 | tf_op jit(solution)/shard_map/ppermute | solution.py:25
  47.2 0.1 add_reduce_fusion.1
  47.3 0.1 multiply_add_fusion.1
  47.5 0.1 broadcast_in_dim.104
  47.6 1.3 %collective-permute-start.3 = (f32[4,136,128]{2,1,0:T(8,128)S(1)}, f32[4,136,128]{2,1,0:T(8,128)S(1)}, u32[]{:S(2)}, u32[]{:S(2)}) collective-permute-start(f32[4,136,128]{2,1,0:T(8,128)S(1)} %pad_maximum_fusion.3), channel_id=1, source_target_pairs={{0,128},{16,144},{32,160},{48,176},{64,192},{80,208},{96,224},{112... | collective-permute-start | bytes 835592 | tf_op jit(solution)/shard_map/ppermute | solution.py:25
  48.9 0.7 copy_bitcast_fusion
  49.6 0.7 convolution_bitcast_fusion.1
  50.3 5.7 %collective-permute-done.3 = f32[4,136,128]{2,1,0:T(8,128)S(1)} collective-permute-done((f32[4,136,128]{2,1,0:T(8,128)S(1)}, f32[4,136,128]{2,1,0:T(8,128)S(1)}, u32[]{:S(2)}, u32[]{:S(2)}) %collective-permute-start.3) | collective-permute-done | bytes 278560 | tf_op jit(solution)/shard_map/ppermute | solution.py:25
  56.0 0.1 exponential_reduce_fusion.1
  56.1 0.1 multiply_add_fusion
  56.3 0.1 broadcast_in_dim.106
  56.4 1.3 %collective-permute-start.4 = (f32[4,136,128]{2,1,0:T(8,128)S(1)}, f32[4,136,128]{2,1,0:T(8,128)S(1)}, u32[]{:S(2)}, u32[]{:S(2)}) collective-permute-start(f32[4,136,128]{2,1,0:T(8,128)S(1)} %pad_maximum_fusion.4), channel_id=1, source_target_pairs={{0,256},{16,272},{32,288},{48,304},{64,320},{80,336},{96,352},{112... | collective-permute-start | bytes 835592 | tf_op jit(solution)/shard_map/ppermute | solution.py:25
  57.7 0.6 fusion.1
  58.3 8.0 %collective-permute-done.4 = f32[4,136,128]{2,1,0:T(8,128)S(1)} collective-permute-done((f32[4,136,128]{2,1,0:T(8,128)S(1)}, f32[4,136,128]{2,1,0:T(8,128)S(1)}, u32[]{:S(2)}, u32[]{:S(2)}) %collective-permute-start.4) | collective-permute-done | bytes 278560 | tf_op jit(solution)/shard_map/ppermute | solution.py:25
  66.3 0.8 multiply_reduce_fusion
  67.1 0.2 copy.76
  67.3 4.9 %psum.21 = f32[256]{0:T(256)S(1)} all-reduce(f32[256]{0:T(256)S(1)} %get-tuple-element.51), channel_id=1, replica_groups=mesh['ctx'=32,'head_hi'=4,'head_2'=2,'head_1'=2] {'head_1'}, use_global_device_ids=true, to_apply=%region_3.4 | all-reduce | flops 256 | bytes 2048 | tf_op jit(solution)/shard_map/psum | solution.py:81
  72.3 5.8 %psum.22 = f32[256]{0:T(256)S(1)} all-reduce(f32[256]{0:T(256)S(1)} %psum.21), channel_id=1, replica_groups=mesh['ctx'=32,'head_hi'=4,'head_2'=2,'head_1'=2] {'head_2'}, use_global_device_ids=true, to_apply=%region_4.5 | all-reduce | flops 256 | bytes 2048 | tf_op jit(solution)/shard_map/psum | solution.py:81
  78.1 23.6 %psum.23 = f32[256]{0:T(256)S(1)} all-reduce(f32[256]{0:T(256)S(1)} %psum.22), channel_id=1, replica_groups=mesh['ctx'=32,'head_hi'=4,'head_2'=2,'head_1'=2] {'head_hi'}, use_global_device_ids=true, to_apply=%region_5.6 | all-reduce | flops 256 | bytes 2048 | tf_op jit(solution)/shard_map/psum | solution.py:81
  101.7 0.8 multiply_convert_fusion
  102.5 18.6 %shard_map.95 = bf16[256,512]{1,0:T(8,128)(2,1)} custom-call(s32[1]{0:T(128)} %bitcast.11.index_ref, bf16[1024,128]{1,0:T(8,128)(2,1)} %bitcast.84, bf16[256,8192]{1,0:T(8,128)(2,1)} %bitcast.82), custom_call_target="tpu_custom_call" | custom-call | tf_op jit(solution)/shard_map/pallas_call | solution.py:145
  (21 shorter events, 0.2 us)
Async XLA Ops:
  7.2 42.4 %copy-start = (bf16[256,512]{1,0:T(8,128)(2,1)S(1)}, bf16[256,512]{1,0:T(8,128)(2,1)}, u32[]{:S(2)}) copy-start(bf16[256,512]{1,0:T(8,128)(2,1)} %param.8) | copy-start | bytes 786436
  7.2 41.7 %copy-start.1 = (bf16[256,512]{1,0:T(8,128)(2,1)S(1)}, bf16[256,512]{1,0:T(8,128)(2,1)}, u32[]{:S(2)}) copy-start(bf16[256,512]{1,0:T(8,128)(2,1)} %param.13) | copy-start | bytes 786436
  7.2 95.3 %all-gather.2.cloned.1.call-start = ((), (), s32[]{:S(2)}) async-start(), calls=%async_computation | async-start | bytes 4325376 | tf_op jit(solution)/shard_map/all_gather | solution.py:171
  14.1 10.0 %collective-permute-start = (f32[4,136,128]{2,1,0:T(8,128)S(1)}, f32[4,136,128]{2,1,0:T(8,128)S(1)}, u32[]{:S(2)}, u32[]{:S(2)}) collective-permute-start(f32[4,136,128]{2,1,0:T(8,128)S(1)} %pad_maximum_fusion), channel_id=1, source_target_pairs={{0,16},{16,32},{32,48},{48,64},{64,80},{80,96},{96,112},{112,128},... | collective-permute-start | bytes 835592 | tf_op jit(solution)/shard_map/ppermute | solution.py:25
  24.2 33.5 %copy-start.2 = (bf16[256,512]{1,0:T(8,128)(2,1)S(1)}, bf16[256,512]{1,0:T(8,128)(2,1)}, u32[]{:S(2)}) copy-start(bf16[256,512]{1,0:T(8,128)(2,1)} %param.10) | copy-start | bytes 786436
  24.4 10.6 %collective-permute-start.1 = (f32[4,136,128]{2,1,0:T(8,128)S(1)}, f32[4,136,128]{2,1,0:T(8,128)S(1)}, u32[]{:S(2)}, u32[]{:S(2)}) collective-permute-start(f32[4,136,128]{2,1,0:T(8,128)S(1)} %pad_maximum_fusion.1), channel_id=1, source_target_pairs={{0,32},{16,48},{32,64},{48,80},{64,96},{80,112},{96,128},{112,144}... | collective-permute-start | bytes 835592 | tf_op jit(solution)/shard_map/ppermute | solution.py:25
  35.3 12.0 %collective-permute-start.2 = (f32[4,136,128]{2,1,0:T(8,128)S(1)}, f32[4,136,128]{2,1,0:T(8,128)S(1)}, u32[]{:S(2)}, u32[]{:S(2)}) collective-permute-start(f32[4,136,128]{2,1,0:T(8,128)S(1)} %pad_maximum_fusion.2), channel_id=1, source_target_pairs={{0,64},{16,80},{32,96},{48,112},{64,128},{80,144},{96,160},{112,17... | collective-permute-start | bytes 835592 | tf_op jit(solution)/shard_map/ppermute | solution.py:25
  47.6 8.4 %collective-permute-start.3 = (f32[4,136,128]{2,1,0:T(8,128)S(1)}, f32[4,136,128]{2,1,0:T(8,128)S(1)}, u32[]{:S(2)}, u32[]{:S(2)}) collective-permute-start(f32[4,136,128]{2,1,0:T(8,128)S(1)} %pad_maximum_fusion.3), channel_id=1, source_target_pairs={{0,128},{16,144},{32,160},{48,176},{64,192},{80,208},{96,224},{112... | collective-permute-start | bytes 835592 | tf_op jit(solution)/shard_map/ppermute | solution.py:25
  49.6 52.1 %copy-start.3 = (f32[512]{0:T(512)S(1)}, f32[512]{0:T(512)}, u32[]{:S(2)}) copy-start(f32[512]{0:T(512)} %param.12) | copy-start | bytes 6148
  56.4 9.9 %collective-permute-start.4 = (f32[4,136,128]{2,1,0:T(8,128)S(1)}, f32[4,136,128]{2,1,0:T(8,128)S(1)}, u32[]{:S(2)}, u32[]{:S(2)}) collective-permute-start(f32[4,136,128]{2,1,0:T(8,128)S(1)} %pad_maximum_fusion.4), channel_id=1, source_target_pairs={{0,256},{16,272},{32,288},{48,304},{64,320},{80,336},{96,352},{112... | collective-permute-start | bytes 835592 | tf_op jit(solution)/shard_map/ppermute | solution.py:25
Sparse Core Ops, SparseCore 0:
  11.6 72.3 all-gather.1

commit v4 on v0

--- a/solution.py
+++ b/solution.py
@@ -11,11 +11,12 @@
 DH = 128
 KV_HEADS = 8
 BLOCK = 256
-KEY_BLOCK = 512
+KEY_BLOCK = 1024
 HEAD_AXES = ("head_hi", "head_lo")
 
 
 EPSILON = 1e-06
+LOG2E = 1.4426950408889634
 NEGATIVE = -1e30
 
 
@@ -98,7 +99,7 @@
         values_t = kvt_ref[DH : 2 * DH, pl.ds(start, KEY_BLOCK)]
         scores = lax.dot_general(
             keys_t, q_ref[...], (((0,), (1,)), ((), ())), preferred_element_type=jnp.float32
-        ) * DH ** (-0.5)
+        ) * (DH ** (-0.5) * LOG2E)
         if masked:
             key_pos = start + lax.broadcasted_iota(jnp.int32, (KEY_BLOCK, wide), 0)
             query_pos = my_index * row_count + lax.rem(
@@ -108,10 +109,10 @@
             scores = jnp.where(allowed, scores, NEGATIVE)
         row_max = max_ref[...]
         new_max = jnp.maximum(row_max, jnp.max(scores, axis=0, keepdims=True))
-        probabilities = jnp.exp(scores - new_max)
+        probabilities = jnp.exp2(scores - new_max)
         if masked:
             probabilities = jnp.where(allowed, probabilities, 0.0)
-        rescale = jnp.exp(row_max - new_max)
+        rescale = jnp.exp2(row_max - new_max)
         total_ref[...] = total_ref[...] * rescale + jnp.sum(probabilities, axis=0, keepdims=True)
         product = jnp.dot(
             values_t, probabilities.astype(jnp.bfloat16), preferred_element_type=jnp.float32

time: 128 us -> 127 us (level)
  Pallas kernels: 18.6 us -> 17.2 us
    pallas_call x1, Pallas kernels: 18.6 us -> 17.2 us  [soft_attention(): pl.pallas_call(soft_kernel, out_shape=jax.ShapeDtypeStruct((row_count, wi...]
where the time goes in v4:
time: 127 us; the launch traced here: 126 us
  waiting for transfers between devices  40.4 us (32%)
  blocking collectives  33.6 us (26%)
  Pallas kernels  17.2 us (14%)
  between operations  14.3 us (11%)
  starting transfers between devices  8.38 us (7%)
  local copies, waits for them, and re-layouts  4.7 us (4%)
  other arithmetic  3.97 us (3%)
  matrix products  3.28 us (3%)
    ppermute x5, waiting for transfers between devices, shifted(): lax.ppermute(value, axis, [(source, source + steps) for source in range(f...  40.4 us
    psum x1, blocking collectives, split_sum(): return lax.psum(partial, 'head_hi')  21.3 us
    pallas_call x1, Pallas kernels, soft_attention(): pl.pallas_call(soft_kernel, out_shape=jax.ShapeDtypeStruct((row_count, wi...  17.2 us
    psum x1, blocking collectives, split_sum(): partial = lax.optimization_barrier(lax.psum(value, 'head_lo'))  12.3 us
    ppermute x5, starting transfers between devices, shifted(): lax.ppermute(value, axis, [(source, source + steps) for source in range(f...  8.35 us
  transfers between devices with their start and end apart: 6, of which 5 were waited for; matrix products, arithmetic and copies ran while one was open for 8% of the time, Pallas kernels for 0%

profile of v4, /device:TPU:6, one launch (start us, length us, event | category | flops | bytes accessed | tf_op | source)
XLA Modules:
  0.0 125.8 jit_solution(1805143156957485899)
XLA Ops:
  7.2 0.0 all-gather.2.cloned.1.call-start
  7.3 0.9 constant_dynamic-slice_fusion
  8.2 0.1 copy.81
  8.3 0.1 copy.82
  8.4 0.7 pad_maximum_fusion.5
  9.1 0.0 all-gather.2.cloned.1.call-update
  9.1 0.7 reshape.90
  9.8 1.2 reduce-window.6
  11.0 0.1 slice.49
  11.1 0.1 copy.65
  11.2 0.1 copy.66
  11.3 0.1 add_bitcast_fusion
  11.4 1.1 copy.83
  12.5 0.2 fusion.37
  12.7 0.1 subtract_exponential_fusion
  12.8 1.2 convolution_add_fusion
  14.0 0.1 broadcast_in_dim.98
  14.1 1.9 %collective-permute-start = (f32[4,136,128]{2,1,0:T(8,128)S(1)}, f32[4,136,128]{2,1,0:T(8,128)S(1)}, u32[]{:S(2)}, u32[]{:S(2)}) collective-permute-start(f32[4,136,128]{2,1,0:T(8,128)S(1)} %pad_maximum_fusion), channel_id=1, source_target_pairs={{0,16},{16,32},{32,48},{48,64},{64,80},{80,96},{96,112},{112,128},... | collective-permute-start | bytes 835592 | tf_op jit(solution)/shard_map/ppermute | solution.py:26
  16.0 8.0 %collective-permute-done = f32[4,136,128]{2,1,0:T(8,128)S(1)} collective-permute-done((f32[4,136,128]{2,1,0:T(8,128)S(1)}, f32[4,136,128]{2,1,0:T(8,128)S(1)}, u32[]{:S(2)}, u32[]{:S(2)}) %collective-permute-start) | collective-permute-done | bytes 278560 | tf_op jit(solution)/shard_map/ppermute | solution.py:26
  24.0 0.1 exponential_reduce_fusion.3
  24.2 0.1 multiply_add_fusion.3
  24.3 0.1 broadcast_in_dim.100
  24.4 1.9 %collective-permute-start.1 = (f32[4,136,128]{2,1,0:T(8,128)S(1)}, f32[4,136,128]{2,1,0:T(8,128)S(1)}, u32[]{:S(2)}, u32[]{:S(2)}) collective-permute-start(f32[4,136,128]{2,1,0:T(8,128)S(1)} %pad_maximum_fusion.1), channel_id=1, source_target_pairs={{0,32},{16,48},{32,64},{48,80},{64,96},{80,112},{96,128},{112,144}... | collective-permute-start | bytes 835592 | tf_op jit(solution)/shard_map/ppermute | solution.py:26
  26.3 8.6 %collective-permute-done.1 = f32[4,136,128]{2,1,0:T(8,128)S(1)} collective-permute-done((f32[4,136,128]{2,1,0:T(8,128)S(1)}, f32[4,136,128]{2,1,0:T(8,128)S(1)}, u32[]{:S(2)}, u32[]{:S(2)}) %collective-permute-start.1) | collective-permute-done | bytes 278560 | tf_op jit(solution)/shard_map/ppermute | solution.py:26
  34.9 0.1 exponential_reduce_fusion.2
  35.0 0.1 multiply_add_fusion.2
  35.2 0.1 broadcast_in_dim.102
  35.3 1.9 %collective-permute-start.2 = (f32[4,136,128]{2,1,0:T(8,128)S(1)}, f32[4,136,128]{2,1,0:T(8,128)S(1)}, u32[]{:S(2)}, u32[]{:S(2)}) collective-permute-start(f32[4,136,128]{2,1,0:T(8,128)S(1)} %pad_maximum_fusion.2), channel_id=1, source_target_pairs={{0,64},{16,80},{32,96},{48,112},{64,128},{80,144},{96,160},{112,17... | collective-permute-start | bytes 835592 | tf_op jit(solution)/shard_map/ppermute | solution.py:26
  37.2 10.1 %collective-permute-done.2 = f32[4,136,128]{2,1,0:T(8,128)S(1)} collective-permute-done((f32[4,136,128]{2,1,0:T(8,128)S(1)}, f32[4,136,128]{2,1,0:T(8,128)S(1)}, u32[]{:S(2)}, u32[]{:S(2)}) %collective-permute-start.2) | collective-permute-done | bytes 278560 | tf_op jit(solution)/shard_map/ppermute | solution.py:26
  47.2 0.1 add_reduce_fusion.1
  47.4 0.1 multiply_add_fusion.1
  47.5 0.1 broadcast_in_dim.104
  47.6 1.3 %collective-permute-start.3 = (f32[4,136,128]{2,1,0:T(8,128)S(1)}, f32[4,136,128]{2,1,0:T(8,128)S(1)}, u32[]{:S(2)}, u32[]{:S(2)}) collective-permute-start(f32[4,136,128]{2,1,0:T(8,128)S(1)} %pad_maximum_fusion.3), channel_id=1, source_target_pairs={{0,128},{16,144},{32,160},{48,176},{64,192},{80,208},{96,224},{112... | collective-permute-start | bytes 835592 | tf_op jit(solution)/shard_map/ppermute | solution.py:26
  48.9 0.7 copy_bitcast_fusion
  49.6 0.7 convolution_bitcast_fusion.1
  50.4 5.7 %collective-permute-done.3 = f32[4,136,128]{2,1,0:T(8,128)S(1)} collective-permute-done((f32[4,136,128]{2,1,0:T(8,128)S(1)}, f32[4,136,128]{2,1,0:T(8,128)S(1)}, u32[]{:S(2)}, u32[]{:S(2)}) %collective-permute-start.3) | collective-permute-done | bytes 278560 | tf_op jit(solution)/shard_map/ppermute | solution.py:26
  56.0 0.1 exponential_reduce_fusion.1
  56.1 0.1 multiply_add_fusion
  56.3 0.1 broadcast_in_dim.106
  56.4 1.3 %collective-permute-start.4 = (f32[4,136,128]{2,1,0:T(8,128)S(1)}, f32[4,136,128]{2,1,0:T(8,128)S(1)}, u32[]{:S(2)}, u32[]{:S(2)}) collective-permute-start(f32[4,136,128]{2,1,0:T(8,128)S(1)} %pad_maximum_fusion.4), channel_id=1, source_target_pairs={{0,256},{16,272},{32,288},{48,304},{64,320},{80,336},{96,352},{112... | collective-permute-start | bytes 835592 | tf_op jit(solution)/shard_map/ppermute | solution.py:26
  57.7 0.6 fusion.1
  58.3 8.0 %collective-permute-done.4 = f32[4,136,128]{2,1,0:T(8,128)S(1)} collective-permute-done((f32[4,136,128]{2,1,0:T(8,128)S(1)}, f32[4,136,128]{2,1,0:T(8,128)S(1)}, u32[]{:S(2)}, u32[]{:S(2)}) %collective-permute-start.4) | collective-permute-done | bytes 278560 | tf_op jit(solution)/shard_map/ppermute | solution.py:26
  66.3 0.8 multiply_reduce_fusion
  67.1 0.2 copy.76
  67.3 12.3 %psum.14 = f32[256]{0:T(256)S(1)} all-reduce(f32[256]{0:T(256)S(1)} %get-tuple-element.51), channel_id=1, replica_groups=mesh['ctx'=32,'head_hi'=4,'head_lo'=4] {'head_lo'}, use_global_device_ids=true, to_apply=%region_3.4 | all-reduce | flops 256 | bytes 2048 | tf_op jit(solution)/shard_map/psum | solution.py:81
  79.6 21.3 %psum.15 = f32[256]{0:T(256)S(1)} all-reduce(f32[256]{0:T(256)S(1)} %psum.14), channel_id=1, replica_groups=mesh['ctx'=32,'head_hi'=4,'head_lo'=4] {'head_hi'}, use_global_device_ids=true, to_apply=%region_4.5 | all-reduce | flops 256 | bytes 2048 | tf_op jit(solution)/shard_map/psum | solution.py:82
  100.9 0.8 multiply_convert_fusion
  101.7 17.2 %shard_map.95 = bf16[256,512]{1,0:T(8,128)(2,1)} custom-call(s32[1]{0:T(128)} %bitcast.11.index_ref, bf16[1024,128]{1,0:T(8,128)(2,1)} %bitcast.84, bf16[256,8192]{1,0:T(8,128)(2,1)} %bitcast.82), custom_call_target="tpu_custom_call" | custom-call | tf_op jit(solution)/shard_map/pallas_call | solution.py:145
  (20 shorter events, 0.2 us)
Async XLA Ops:
  7.2 42.4 %copy-start = (bf16[256,512]{1,0:T(8,128)(2,1)S(1)}, bf16[256,512]{1,0:T(8,128)(2,1)}, u32[]{:S(2)}) copy-start(bf16[256,512]{1,0:T(8,128)(2,1)} %param.8) | copy-start | bytes 786436
  7.2 41.7 %copy-start.1 = (bf16[256,512]{1,0:T(8,128)(2,1)S(1)}, bf16[256,512]{1,0:T(8,128)(2,1)}, u32[]{:S(2)}) copy-start(bf16[256,512]{1,0:T(8,128)(2,1)} %param.13) | copy-start | bytes 786436
  7.2 94.5 %all-gather.2.cloned.1.call-start = ((), (), s32[]{:S(2)}) async-start(), calls=%async_computation | async-start | bytes 4325376 | tf_op jit(solution)/shard_map/all_gather | solution.py:171
  14.1 10.0 %collective-permute-start = (f32[4,136,128]{2,1,0:T(8,128)S(1)}, f32[4,136,128]{2,1,0:T(8,128)S(1)}, u32[]{:S(2)}, u32[]{:S(2)}) collective-permute-start(f32[4,136,128]{2,1,0:T(8,128)S(1)} %pad_maximum_fusion), channel_id=1, source_target_pairs={{0,16},{16,32},{32,48},{48,64},{64,80},{80,96},{96,112},{112,128},... | collective-permute-start | bytes 835592 | tf_op jit(solution)/shard_map/ppermute | solution.py:26
  24.2 33.6 %copy-start.2 = (bf16[256,512]{1,0:T(8,128)(2,1)S(1)}, bf16[256,512]{1,0:T(8,128)(2,1)}, u32[]{:S(2)}) copy-start(bf16[256,512]{1,0:T(8,128)(2,1)} %param.10) | copy-start | bytes 786436
  24.4 10.6 %collective-permute-start.1 = (f32[4,136,128]{2,1,0:T(8,128)S(1)}, f32[4,136,128]{2,1,0:T(8,128)S(1)}, u32[]{:S(2)}, u32[]{:S(2)}) collective-permute-start(f32[4,136,128]{2,1,0:T(8,128)S(1)} %pad_maximum_fusion.1), channel_id=1, source_target_pairs={{0,32},{16,48},{32,64},{48,80},{64,96},{80,112},{96,128},{112,144}... | collective-permute-start | bytes 835592 | tf_op jit(solution)/shard_map/ppermute | solution.py:26
  35.3 12.0 %collective-permute-start.2 = (f32[4,136,128]{2,1,0:T(8,128)S(1)}, f32[4,136,128]{2,1,0:T(8,128)S(1)}, u32[]{:S(2)}, u32[]{:S(2)}) collective-permute-start(f32[4,136,128]{2,1,0:T(8,128)S(1)} %pad_maximum_fusion.2), channel_id=1, source_target_pairs={{0,64},{16,80},{32,96},{48,112},{64,128},{80,144},{96,160},{112,17... | collective-permute-start | bytes 835592 | tf_op jit(solution)/shard_map/ppermute | solution.py:26
  47.6 8.4 %collective-permute-start.3 = (f32[4,136,128]{2,1,0:T(8,128)S(1)}, f32[4,136,128]{2,1,0:T(8,128)S(1)}, u32[]{:S(2)}, u32[]{:S(2)}) collective-permute-start(f32[4,136,128]{2,1,0:T(8,128)S(1)} %pad_maximum_fusion.3), channel_id=1, source_target_pairs={{0,128},{16,144},{32,160},{48,176},{64,192},{80,208},{96,224},{112... | collective-permute-start | bytes 835592 | tf_op jit(solution)/shard_map/ppermute | solution.py:26
  49.6 51.3 %copy-start.3 = (f32[512]{0:T(512)S(1)}, f32[512]{0:T(512)}, u32[]{:S(2)}) copy-start(f32[512]{0:T(512)} %param.12) | copy-start | bytes 6148
  56.4 9.9 %collective-permute-start.4 = (f32[4,136,128]{2,1,0:T(8,128)S(1)}, f32[4,136,128]{2,1,0:T(8,128)S(1)}, u32[]{:S(2)}, u32[]{:S(2)}) collective-permute-start(f32[4,136,128]{2,1,0:T(8,128)S(1)} %pad_maximum_fusion.4), channel_id=1, source_target_pairs={{0,256},{16,272},{32,288},{48,304},{64,320},{80,336},{96,352},{112... | collective-permute-start | bytes 835592 | tf_op jit(solution)/shard_map/ppermute | solution.py:26
Sparse Core Ops, SparseCore 0:
  11.6 72.3 all-gather.1
